TPU v7x, 256 devices: a whole 4x4x8 slice. The times are simulated.
256 devices in a mesh: req: 64 (over z, x, core), tp: 4 (over y).
Axes of the slice: x: 4, y: 4, z: 8, core: 2. Of those that a mesh axis runs over, the one named last changes fastest.
Arguments:
- hidden: bfloat16 [16384, 2048], P('req'), may hold values from -10.5 to 10.5
- lengths: int32 [64], replicated, may hold values from 1 to 1024, 16384 in all
- dealing: int32 [64], replicated, may hold values from 0 to 63, each once
- norm_gain: bfloat16 [2048], replicated, may hold values from 0.5 to 1.5
- w_query: bfloat16 [2048, 2048], P(None, 'tp'), may hold values from -0.125 to 0.125
- w_key: bfloat16 [2048, 1024], P(None, 'tp'), may hold values from -0.125 to 0.125
- w_value: bfloat16 [2048, 1024], P(None, 'tp'), may hold values from -0.125 to 0.125
- query_gain: bfloat16 [128], replicated, may hold values from 0.5 to 8
- key_gain: bfloat16 [128], replicated, may hold values from 0.5 to 8
- w_out: bfloat16 [2048, 2048], P(None, 'tp'), may hold values from -0.125 to 0.125
Outputs:
- hidden_out: bfloat16 [16384, 2048], P('req', 'tp')
- kv_cache: bfloat16 [2, 64, 1024, 1024], P(None, 'req', None, 'tp')
Inputs may be any that keep to these rules, and one draw needn't show every extreme that they name: The lengths sum to 16384; the largest is exactly 1024. A permutation: dealt slot j, on device j of req, holds prompt dealing[j].
All inputs are finite; a program needn't handle non-finite values.
Results may differ from a plain program's by a relative error of at most 0.012.
The roundings to bfloat16 on the way count: a program that leaves them out, or rounds other values in their place, can miss the bound.
Values may be sent and summed in bfloat16 or wider, within the bound.
No kernel may reach another device: no remote copies, remote signals or barrier semaphores. Data moves between devices by JAX's collectives and lax.ppermute only.
A program may use at most 128 MiB of HBM per device.

v0:
```python
import jax
import jax.numpy as jnp
from jax import lax
from jax.sharding import PartitionSpec as P

EPS = 1e-06
THETA = 1000000.0


def rms_rows(values, scale_gain):
    inv_rms = lax.rsqrt(jnp.mean(values * values, axis=-1, keepdims=True) + EPS)
    return values * inv_rms * scale_gain


def rotate(values, positions):
    features = values.shape[-1]
    half_width = features // 2
    frequency = THETA ** (-(jnp.arange(half_width).astype(jnp.float32) * 2.0) / features)
    angles = positions.astype(jnp.float32)[:, None] * frequency[None, :]
    cosine = jnp.cos(angles)[:, None, :]
    sine_part = jnp.sin(angles)[:, None, :]
    first_half = values[..., :half_width]
    second_half = values[..., half_width:]
    return jnp.concatenate(
        [
            first_half * cosine - second_half * sine_part,
            second_half * cosine + first_half * sine_part,
        ],
        axis=-1,
    )


def project(normed, w_query, w_key, w_value, query_gain, key_gain, positions):
    head_dim = query_gain.shape[0]
    row_count = normed.shape[0]
    query_rows = jnp.dot(normed, w_query, preferred_element_type=jnp.float32).reshape(
        row_count, -1, head_dim
    )
    key_rows = jnp.dot(normed, w_key, preferred_element_type=jnp.float32).reshape(
        row_count, -1, head_dim
    )
    value_rows = jnp.dot(normed, w_value, preferred_element_type=jnp.float32).astype(jnp.bfloat16)
    query_rows = rotate(rms_rows(query_rows, query_gain.astype(jnp.float32)), positions).astype(
        jnp.bfloat16
    )
    key_rows = rotate(rms_rows(key_rows, key_gain.astype(jnp.float32)), positions).astype(
        jnp.bfloat16
    )
    return (query_rows.reshape(row_count, -1), key_rows.reshape(row_count, -1), value_rows)


def attend(query_slot, key_slot, value_slot, prompt_length, head_dim):
    slot_len, query_width = query_slot.shape
    kv_heads = key_slot.shape[1] // head_dim
    group_size = query_width // head_dim // kv_heads
    queries = query_slot.reshape(slot_len, kv_heads, group_size, head_dim)
    keys_split = key_slot.reshape(slot_len, kv_heads, head_dim)
    values_split = value_slot.reshape(slot_len, kv_heads, head_dim)
    scores = jnp.einsum(
        "qkgd,skd->kgqs", queries, keys_split, preferred_element_type=jnp.float32
    ) * head_dim ** (-0.5)
    offsets = jnp.arange(slot_len, dtype=jnp.int32)
    allowed = (offsets[None, :] <= offsets[:, None]) & (offsets[None, :] < prompt_length)
    scores = jnp.where(allowed[None, None], scores, -jnp.inf)
    row_max = jnp.max(scores, axis=-1, keepdims=True)
    weights = jnp.exp(scores - row_max)
    weights = (weights / jnp.sum(weights, axis=-1, keepdims=True)).astype(jnp.bfloat16)
    mixture = jnp.einsum(
        "kgqs,skd->qkgd", weights, values_split, preferred_element_type=jnp.float32
    )
    return mixture.astype(jnp.bfloat16).reshape(slot_len, query_width)


def on_device(
    hidden, lengths, dealing, norm_gain, w_query, w_key, w_value, query_gain, key_gain, w_out
):
    devices = lax.axis_size("req")
    home_index = lax.axis_index("req")
    slice_index = lax.axis_index("tp")
    tok_rows, features = hidden.shape
    head_dim = query_gain.shape[0]
    out_width = w_out.shape[1]
    q_width = w_query.shape[1]
    k_width = w_key.shape[1]
    slot_len = 4 * tok_rows
    capacity = slot_len // devices
    prompt_total = lengths.shape[0]
    prompt_ids = jnp.arange(prompt_total, dtype=jnp.int32)
    prompt_ends = jnp.cumsum(lengths)
    starts = prompt_ends - lengths
    packed_ids = jnp.arange(tok_rows, dtype=jnp.int32) * devices + home_index
    segment = jnp.sum((packed_ids[:, None] >= prompt_ends[None, :]).astype(jnp.int32), axis=1)
    seg_onehot = (segment[:, None] == prompt_ids[None, :]).astype(jnp.int32)
    positions = packed_ids - jnp.sum(seg_onehot * starts[None, :], axis=1)
    inverse = jnp.zeros((prompt_total,), jnp.int32).at[dealing].set(prompt_ids)
    deal_hot = (dealing[:, None] == prompt_ids[None, :]).astype(jnp.int32)
    dealt_starts = jnp.sum(deal_hot * starts[None, :], axis=1)
    dealt_lengths = jnp.sum(deal_hot * lengths[None, :], axis=1)
    first_offset = jnp.mod(home_index - dealt_starts, devices)
    ranks = jnp.arange(capacity, dtype=jnp.int32)
    slot_offset = first_offset[None, :] + ranks[:, None] * devices
    send_valid = slot_offset < dealt_lengths[None, :]
    send_rows = jnp.where(
        send_valid, (dealt_starts[None, :] + slot_offset - home_index) // devices, 0
    ).reshape(-1)
    my_start = lax.dynamic_index_in_dim(dealt_starts, home_index, 0, keepdims=False)
    my_length = lax.dynamic_index_in_dim(dealt_lengths, home_index, 0, keepdims=False)
    roll_shift = jnp.mod(my_start, devices)
    my_slots = jnp.sum(seg_onehot * inverse[None, :], axis=1)
    back_rows = positions // devices * devices + my_slots
    gain_values = norm_gain.astype(jnp.float32)
    normed = rms_rows(hidden.astype(jnp.float32), gain_values).astype(jnp.bfloat16)
    query_rows, key_rows, value_rows = project(
        normed, w_query, w_key, w_value, query_gain, key_gain, positions
    )
    qkv_rows = jnp.concatenate([query_rows, key_rows, value_rows], axis=1)
    picked = jnp.take(qkv_rows, send_rows, axis=0).reshape(capacity, devices, qkv_rows.shape[1])
    arrived = lax.all_to_all(
        jnp.where(send_valid[:, :, None], picked, jnp.zeros((), qkv_rows.dtype)),
        "req",
        split_axis=1,
        concat_axis=1,
        tiled=True,
    )
    slot_rows = jnp.roll(arrived, -roll_shift, axis=1).reshape(slot_len, arrived.shape[2])
    query_slot = slot_rows[:, :q_width]
    key_slot = slot_rows[:, q_width : q_width + k_width]
    value_slot = slot_rows[:, q_width + k_width :]
    mixture = attend(query_slot, key_slot, value_slot, my_length, head_dim)
    sendback = jnp.roll(mixture.reshape(capacity, devices, mixture.shape[1]), roll_shift, axis=1)
    returned = lax.all_to_all(sendback, "req", split_axis=1, concat_axis=1, tiled=True)
    attended = jnp.take(returned.reshape(capacity * devices, -1), back_rows, axis=0)
    kv_cache = jnp.stack([key_slot, value_slot])[:, None]
    summed = jnp.dot(
        lax.all_gather(attended, "tp", axis=1, tiled=True),
        w_out,
        preferred_element_type=jnp.float32,
    )
    branch = lax.optimization_barrier(summed.astype(jnp.bfloat16))
    residual = lax.dynamic_slice_in_dim(hidden, slice_index * out_width, out_width, 1)
    hidden_out = (residual.astype(jnp.float32) + branch.astype(jnp.float32)).astype(jnp.bfloat16)
    return (hidden_out, kv_cache)


def solution(mesh):
    in_specs = (
        P("req", None),
        P(),
        P(),
        P(),
        P(None, "tp"),
        P(None, "tp"),
        P(None, "tp"),
        P(),
        P(),
        P(None, "tp"),
    )
    out_specs = (P("req", "tp"), P(None, "req", None, "tp"))
    return jax.shard_map(
        on_device, mesh=mesh, in_specs=in_specs, out_specs=out_specs, check_vma=False
    )
```

profile of v0, /device:TPU:2, one launch (start us, length us, event | category | flops | bytes accessed | tf_op | source)
XLA Modules:
  0.0 212.4 jit_solution(9252795499204256088)
XLA Ops:
  7.2 0.9 copy.123
  8.1 0.1 reduce-window.8
  8.2 0.1 reduce
  8.3 0.7 sub.88
  9.0 0.8 select_reduce_fusion.2
  9.8 0.7 compare_select_fusion.7
  10.5 0.1 fusion.17
  10.6 0.6 compare_and_fusion
  11.2 0.7 lt.124
  11.9 0.1 copy.124
  12.0 0.7 convert_element_type.73
  12.7 1.6 fusion.7
  14.3 2.2 %convolution_convert_fusion.1 = bf16[256,256]{0,1:T(8,128)(2,1)S(1)} fusion(bf16[2048,256]{1,0:T(8,128)(2,1)} %param.16, bf16[256,2048]{1,0:T(8,128)(2,1)} %param.10, f32[2048]{0:T(1024)S(1)} %convert_element_type.73, f32[256]{0:T(256)S(1)} %add_rsqrt_fusion.2), kind=kOutput, calls=%fused_computation.30 | convolution fusion | flops 270598144 | bytes 2237440 | tf_op jit(solution)/shard_map/dot_general | solution.py:42
  16.6 0.7 copy.131
  17.3 0.6 convert_element_type.79
  17.9 2.6 %multiply_reduce_fusion.1 = (f32[256,2]{0,1:T(2,128)S(1)}, f32[256,256]{0,1:T(8,128)}) fusion(bf16[2048,256]{1,0:T(8,128)(2,1)} %param.15, bf16[256,2048]{1,0:T(8,128)(2,1)S(1)} %copy-done.1, f32[2048]{0:T(1024)S(1)} %convert_element_type.73, f32[256]{0:T(256)S(1)} %add_rsqrt_fusion.2), kind=kOutput, calls=%fused_computation.42 | convolution fusion | flops 270663168 | bytes 2370560 | tf_op jit(solution)/shard_map/dot_general | solution.py:39
  20.5 0.6 add_rsqrt_fusion.1
  21.0 0.1 convert_reduce_fusion
  21.1 0.8 scatter_custom_fusion
  21.9 0.6 select_reduce_fusion
  22.6 0.6 copy-done.5
  23.1 0.3 multiply_cosine_fusion
  23.5 0.1 copy.129
  23.6 0.1 copy.128
  23.7 1.1 multiply_multiply_fusion.1
  24.8 0.8 copy.149
  25.6 2.3 %fusion.29 = f32[256,512]{1,0:T(8,128)} fusion(bf16[2048,512]{1,0:T(8,128)(2,1)S(1)} %copy-done, bf16[256,2048]{1,0:T(8,128)(2,1)S(1)} %copy-done.1, f32[2048]{0:T(1024)} %copy-done.9, f32[256]{0:T(256)} %copy-done.14), kind=kOutput, calls=%fused_computation.107 | convolution fusion | flops 538968064 | bytes 3679232 | tf_op jit(solution)/shard_map/dot_general | solution.py:36
  27.8 1.2 reshape.456
  29.1 0.3 multiply_reduce_fusion
  29.5 0.3 multiply_multiply_fusion
  29.8 0.5 subtract_convert_fusion
  30.3 0.4 pad_maximum_fusion.1
  30.7 0.1 sub.98
  30.9 0.1 copy.125
  31.1 5.4 %gather_fusion = bf16[1024,1024]{1,0:T(8,128)(2,1)} fusion(bf16[256,1024]{1,0:T(8,128)(2,1)S(1)} %pad_maximum_fusion, s32[1024]{0:T(1024)S(1)} %broadcast_clamp_fusion), kind=kCustom, calls=%fused_computation | custom fusion | bytes 4198400 | tf_op jit(solution)/shard_map/jit(_take)/gather | solution.py:117
  36.5 4.0 %fusion.11 = bf16[16,64,1024]{2,0,1:T(8,128)(2,1)} fusion(bf16[16,64,1024]{2,1,0:T(8,128)(2,1)} %bitcast.61, pred[16,64]{0,1:T(8,128)(4,1)S(1)} %copy.125, pred[16,64]{0,1:T(8,128)(4,1)S(1)} %copy.124), kind=kLoop, calls=%fused_computation.25 | loop fusion | flops 2097152 | bytes 4196352 | tf_op jit(solution)/shard_map/jit(_where)/select_n | solution.py:119
  40.5 12.4 %all-to-all-start = ((bf16[16,64,1024]{2,0,1:T(8,128)(2,1)}), bf16[16,64,1024]{2,0,1:T(8,128)(2,1)}, u32[]{:S(2)}, u32[]{:S(2)}) async-start(bf16[16,64,1024]{2,0,1:T(8,128)(2,1)} %fusion.11), calls=%async_computation | async-start | bytes 4194304 | tf_op jit(solution)/shard_map/all_to_all | solution.py:118
  52.9 0.6 dynamic_slice.19
  55.5 0.6 dynamic_slice.21
  56.1 0.6 iota_compare_fusion.3
  56.7 1.3 fusion.6
  58.0 46.0 %all-to-all-done = bf16[16,64,1024]{2,0,1:T(8,128)(2,1)} async-done(((bf16[16,64,1024]{2,0,1:T(8,128)(2,1)}), bf16[16,64,1024]{2,0,1:T(8,128)(2,1)}, u32[]{:S(2)}, u32[]{:S(2)}) %all-to-all-start) | async-done | bytes 2097184 | tf_op jit(solution)/shard_map/all_to_all | solution.py:118
  104.0 2.7 %copy.133 = bf16[16,64,1024]{2,1,0:T(8,128)(2,1)S(1)} copy(bf16[16,64,1024]{2,0,1:T(8,128)(2,1)} %all-to-all-done) | data formatting | bytes 4194304 | tf_op jit(solution)/shard_map/all_to_all | solution.py:118
  106.8 1.6 fusion.10
  108.4 1.4 slice_bitcast_fusion
  109.8 0.1 slice.38
  109.9 2.0 copy.135
  112.0 2.1 copy.136
  114.0 1.3 copy.137
  115.3 11.2 %fusion.31 = (f32[2,2,1024]{2,1,0:T(2,128)S(1)}, f32[2,2,1024,1024]{2,3,1,0:T(8,128)}) fusion(pred[1024,1024]{0,1:T(8,128)(4,1)} %fusion.6, bf16[1024,2,128,1]{0,2,3,1:T(8,128)(2,1)} %bitcast.68, bf16[1024,2,2,128]{0,3,2,1:T(8,128)(2,1)} %bitcast.65), kind=kOutput, calls=%fused_computation.108 | convolution fusion | flops 1090520064 | bytes 19415040 | tf_op jit(solution)/shard_map/sub | solution.py:66
  126.5 7.2 %fusion.15 = bf16[1024,2,2,128]{0,3,2,1:T(8,128)(2,1)S(1)} fusion(bf16[1024,2,128,1]{0,2,3,1:T(8,128)(2,1)} %bitcast.67, f32[2,2,1024,1024]{2,3,1,0:T(8,128)} %get-tuple-element.35, f32[2,2,1024]{2,1,0:T(2,128)S(1)} %get-tuple-element.34), kind=kOutput, calls=%fused_computation.28 | convolution fusion | flops 1082654720 | bytes 18366464 | tf_op jit(solution)/shard_map/kgqs,skd->qkgd/dot_general | solution.py:68
  133.8 2.0 copy.141
  135.8 1.5 reshape_reshape.3
  137.3 0.8 fusion.16
  138.1 1.5 copy.142
  139.7 5.6 %all-to-all-start.1 = ((bf16[16,64,512]{2,0,1:T(8,128)(2,1)}), bf16[16,64,512]{2,0,1:T(8,128)(2,1)}, u32[]{:S(2)}, u32[]{:S(2)}) async-start(bf16[16,64,512]{2,0,1:T(8,128)(2,1)} %copy.142), calls=%async_computation.1 | async-start | bytes 2097152 | tf_op jit(solution)/shard_map/all_to_all | solution.py:131
  145.4 28.6 %all-to-all-done.1 = bf16[16,64,512]{2,0,1:T(8,128)(2,1)} async-done(((bf16[16,64,512]{2,0,1:T(8,128)(2,1)}), bf16[16,64,512]{2,0,1:T(8,128)(2,1)}, u32[]{:S(2)}, u32[]{:S(2)}) %all-to-all-start.1) | async-done | bytes 1048608 | tf_op jit(solution)/shard_map/all_to_all | solution.py:131
  174.0 1.8 copy.143
  175.8 1.2 gather_fusion.1
  176.9 0.8 broadcast_select_fusion
  177.8 2.3 %maximum_bitcast_fusion = bf16[2,1,1024,256]{3,2,1,0:T(8,128)(2,1)} fusion(bf16[1,1024,256]{2,1,0:T(8,128)(2,1)} %get-tuple-element.21, bf16[1,1024,256]{2,1,0:T(8,128)(2,1)} %get-tuple-element.20), kind=kLoop, calls=%fused_computation.32 | loop fusion | flops 524288 | bytes 2097152
  180.1 21.2 %all-gather.2.cloned.1.call-done = bf16[256,2048]{1,0:T(8,128)(2,1)} async-done(((bf16[256,512]{1,0:T(8,128)(2,1)}), bf16[256,2048]{1,0:T(8,128)(2,1)}) %all-gather.2.cloned.1.call-update) | async-done | bytes 1048592 | tf_op jit(solution)/shard_map/all_gather | solution.py:135
  201.2 2.6 %convolution_convert_fusion = bf16[256,512]{1,0:T(8,128)(2,1)S(1)} fusion(bf16[256,2048]{1,0:T(8,128)(2,1)} %all-gather.2.cloned.1.call-done, bf16[2048,512]{1,0:T(8,128)(2,1)} %param.19), kind=kOutput, calls=%fused_computation.29 | convolution fusion | flops 537001984 | bytes 3407872 | tf_op jit(solution)/shard_map/dot_general | solution.py:134
  203.8 1.7 add_convert_fusion
  (52 shorter events, 0.4 us)
Async XLA Ops:
  7.2 18.4 %copy-start = (bf16[2048,512]{1,0:T(8,128)(2,1)S(1)}, bf16[2048,512]{1,0:T(8,128)(2,1)}, u32[]{:S(2)}) copy-start(bf16[2048,512]{1,0:T(8,128)(2,1)} %param.14) | copy-start | bytes 6291460
  9.8 2.2 %copy-start.10 = (s32[64]{0:T(128)}, s32[64]{0:T(128)S(1)}, u32[]{:S(2)}) copy-start(s32[64]{0:T(128)S(1)} %get-tuple-element.19) | copy-start | bytes 772
  9.8 7.5 %copy-start.12 = (s32[64]{0:T(128)}, s32[64]{0:T(128)S(1)}, u32[]{:S(2)}) copy-start(s32[64]{0:T(128)S(1)} %get-tuple-element.18) | copy-start | bytes 772
  12.7 5.2 %copy-start.9 = (f32[2048]{0:T(1024)}, f32[2048]{0:T(1024)S(1)}, u32[]{:S(2)}) copy-start(f32[2048]{0:T(1024)S(1)} %convert_element_type.73) | copy-start | bytes 24580
  12.7 4.6 %copy-start.15 = (bf16[128]{0:T(256)(128)(2,1)S(1)}, bf16[128]{0:T(256)(128)(2,1)}, u32[]{:S(2)}) copy-start(bf16[128]{0:T(256)(128)(2,1)} %param.18) | copy-start | bytes 772
  12.7 5.2 %copy-start.1 = (bf16[256,2048]{1,0:T(8,128)(2,1)S(1)}, bf16[256,2048]{1,0:T(8,128)(2,1)}, u32[]{:S(2)}) copy-start(bf16[256,2048]{1,0:T(8,128)(2,1)} %param.10) | copy-start | bytes 3145732
  14.3 6.1 %copy-start.14 = (f32[256]{0:T(256)}, f32[256]{0:T(256)S(1)}, u32[]{:S(2)}) copy-start(f32[256]{0:T(256)S(1)} %add_rsqrt_fusion.2) | copy-start | bytes 3076
  22.6 0.6 copy-start.5
  25.6 3.5 %copy-start.16 = (bf16[128]{0:T(256)(128)(2,1)S(1)}, bf16[128]{0:T(256)(128)(2,1)}, u32[]{:S(2)}) copy-start(bf16[128]{0:T(256)(128)(2,1)} %param.17) | copy-start | bytes 772
  29.4 1.4 copy-start.4
  29.4 1.4 copy-start.8
  29.5 1.5 copy-start.2
  29.5 1.5 copy-start.3
  40.5 12.4 %copy-start.11 = (s32[64]{0:T(128)S(1)}, s32[64]{0:T(128)}, u32[]{:S(2)}) copy-start(s32[64]{0:T(128)} %copy-done.10) | copy-start | bytes 772
  40.5 15.0 %copy-start.13 = (s32[64]{0:T(128)S(1)}, s32[64]{0:T(128)}, u32[]{:S(2)}) copy-start(s32[64]{0:T(128)} %copy-done.12) | copy-start | bytes 772
  40.5 63.5 %all-to-all-start = ((bf16[16,64,1024]{2,0,1:T(8,128)(2,1)}), bf16[16,64,1024]{2,0,1:T(8,128)(2,1)}, u32[]{:S(2)}, u32[]{:S(2)}) async-start(bf16[16,64,1024]{2,0,1:T(8,128)(2,1)} %fusion.11), calls=%async_computation | async-start | bytes 4194304 | tf_op jit(solution)/shard_map/all_to_all | solution.py:118
  138.1 7.3 %copy-start.6 = (s32[256]{0:T(256)S(1)}, s32[256]{0:T(256)}, u32[]{:S(2)}) copy-start(s32[256]{0:T(256)} %copy-done.5) | copy-start | bytes 3076
  138.1 7.3 %copy-start.7 = (s32[256]{0:T(256)S(1)}, s32[256]{0:T(256)}, u32[]{:S(2)}) copy-start(s32[256]{0:T(256)} %get-tuple-element.16) | copy-start | bytes 3076
  139.7 34.3 %all-to-all-start.1 = ((bf16[16,64,512]{2,0,1:T(8,128)(2,1)}), bf16[16,64,512]{2,0,1:T(8,128)(2,1)}, u32[]{:S(2)}, u32[]{:S(2)}) async-start(bf16[16,64,512]{2,0,1:T(8,128)(2,1)} %copy.142), calls=%async_computation.1 | async-start | bytes 2097152 | tf_op jit(solution)/shard_map/all_to_all | solution.py:131
  145.3 55.9 %all-gather.2.cloned.1.call-start = ((), (), s32[]{:S(2)}) async-start(), calls=%async_computation.2 | async-start | bytes 1310720 | tf_op jit(solution)/shard_map/all_gather | solution.py:135
Sparse Core Ops, SparseCore 0:
  177.9 23.2 all-gather.1
where the time goes:
time: 213 us; the launch traced here: 212 us
  waiting for transfers between devices  95.7 us (45%)
  local copies, waits for them, and re-layouts  30.5 us (14%)
  matrix products  28.1 us (13%)
  other arithmetic  23.7 us (11%)
  starting transfers between devices  18 us (8%)
  between operations  16.4 us (8%)
    all_to_all x1, waiting for transfers between devices, on_device(): lax.all_to_all(jnp.where(send_valid[:, :, None], picked, jnp.zeros((), qk...  46 us
    all_to_all x1, waiting for transfers between devices, on_device(): lax.all_to_all(sendback, 'req', split_axis=1, concat_axis=1, tiled=True)  28.6 us
    all_gather x1, waiting for transfers between devices, on_device(): lax.all_gather(attended, 'tp', axis=1, tiled=True)  21.2 us
    all_to_all x1, starting transfers between devices, on_device(): lax.all_to_all(jnp.where(send_valid[:, :, None], picked, jnp.zeros((), qk...  12.4 us
    sub x1, matrix products, attend(): weights = jnp.exp(scores - row_max)  11.2 us
    dot_general x1, matrix products, attend(): jnp.einsum('kgqs,skd->qkgd', weights, values_split, preferred_element_typ...  7.24 us
    all_to_all x1, starting transfers between devices, on_device(): lax.all_to_all(sendback, 'req', split_axis=1, concat_axis=1, tiled=True)  5.63 us
    gather x1, local copies, waits for them, and re-layouts, on_device(): jnp.take(qkv_rows, send_rows, axis=0)  5.39 us
  transfers between devices with their start and end apart: 3, of which 3 were waited for; matrix products, arithmetic and copies ran while one was open for 3% of the time, Pallas kernels for 0%

commit v1 on v0

--- a/solution.py
+++ b/solution.py
@@ -2,9 +2,17 @@
 import jax.numpy as jnp
 from jax import lax
 from jax.sharding import PartitionSpec as P
+from jax.lax import all_to_all, axis_size
 
 EPS = 1e-06
 THETA = 1000000.0
+
+
+def _direct_series_all(unit):
+    u1 = jnp.concatenate(
+        all_to_all(jnp.stack([unit for _ in range(axis_size("tp"))]), "tp", 0, 0), axis=1
+    )
+    return u1
 
 
 def rms_rows(values, scale_gain):
@@ -131,11 +139,7 @@
     returned = lax.all_to_all(sendback, "req", split_axis=1, concat_axis=1, tiled=True)
     attended = jnp.take(returned.reshape(capacity * devices, -1), back_rows, axis=0)
     kv_cache = jnp.stack([key_slot, value_slot])[:, None]
-    summed = jnp.dot(
-        lax.all_gather(attended, "tp", axis=1, tiled=True),
-        w_out,
-        preferred_element_type=jnp.float32,
-    )
+    summed = jnp.dot(_direct_series_all(attended), w_out, preferred_element_type=jnp.float32)
     branch = lax.optimization_barrier(summed.astype(jnp.bfloat16))
     residual = lax.dynamic_slice_in_dim(hidden, slice_index * out_width, out_width, 1)
     hidden_out = (residual.astype(jnp.float32) + branch.astype(jnp.float32)).astype(jnp.bfloat16)

time: 213 us -> 198 us (0.930)
  between operations: 16.4 us -> 3.02 us
  waiting for transfers between devices: 95.7 us -> 87.8 us
  starting transfers between devices: 18 us -> 22.4 us
  local copies, waits for them, and re-layouts: 30.5 us -> 32.8 us
    all_gather x1 -> x0, waiting for transfers between devices: 21.2 us -> none  [on_device(): lax.all_gather(attended, 'tp', axis=1, tiled=True)]
    all_to_all x0 -> x1, waiting for transfers between devices: none -> 13.2 us  [_direct_series_all(): all_to_all(jnp.stack([unit for _ in range(axis_size('tp'))]), 'tp', 0, 0)]
    all_to_all x0 -> x1, starting transfers between devices: none -> 4.46 us  [_direct_series_all(): all_to_all(jnp.stack([unit for _ in range(axis_size('tp'))]), 'tp', 0, 0)]
  transfers between devices with their start and end apart: 3 -> 3, of which waited for: 3 -> 3; matrix products, arithmetic and copies ran while one was open for 3% -> 2% of each run, Pallas kernels for 0% -> 0%
where the time goes in v1:
time: 198 us; the launch traced here: 197 us
  waiting for transfers between devices  87.8 us (44%)
  local copies, waits for them, and re-layouts  32.8 us (17%)
  matrix products  28.1 us (14%)
  other arithmetic  22.5 us (11%)
  starting transfers between devices  22.4 us (11%)
  between operations  3.02 us (2%)
    all_to_all x1, waiting for transfers between devices, on_device(): lax.all_to_all(jnp.where(send_valid[:, :, None], picked, jnp.zeros((), qk...  46 us
    all_to_all x1, waiting for transfers between devices, on_device(): lax.all_to_all(sendback, 'req', split_axis=1, concat_axis=1, tiled=True)  28.6 us
    all_to_all x1, waiting for transfers between devices, _direct_series_all(): all_to_all(jnp.stack([unit for _ in range(axis_size('tp'))]), 'tp', 0, 0)  13.2 us
    all_to_all x1, starting transfers between devices, on_device(): lax.all_to_all(jnp.where(send_valid[:, :, None], picked, jnp.zeros((), qk...  12.4 us
    sub x1, matrix products, attend(): weights = jnp.exp(scores - row_max)  11.2 us
    dot_general x1, matrix products, attend(): jnp.einsum('kgqs,skd->qkgd', weights, values_split, preferred_element_typ...  7.24 us
    all_to_all x1, starting transfers between devices, on_device(): lax.all_to_all(sendback, 'req', split_axis=1, concat_axis=1, tiled=True)  5.63 us
    gather x1, local copies, waits for them, and re-layouts, on_device(): jnp.take(qkv_rows, send_rows, axis=0)  5.39 us
  transfers between devices with their start and end apart: 3, of which 3 were waited for; matrix products, arithmetic and copies ran while one was open for 2% of the time, Pallas kernels for 0%

profile of v1, /device:TPU:2, one launch (start us, length us, event | category | flops | bytes accessed | tf_op | source)
XLA Modules:
  0.0 196.6 jit_solution(6020284571209508463)
XLA Ops:
  0.7 0.9 copy.129
  1.6 0.1 reduce-window.8
  1.7 0.1 reduce
  1.8 0.7 sub.88
  2.4 0.8 select_reduce_fusion.2
  3.3 0.7 compare_select_fusion.7
  4.1 0.6 compare_and_fusion
  4.7 0.7 lt.124
  5.4 0.1 copy.130
  5.5 0.7 convert_element_type.73
  6.2 1.6 fusion.7
  7.8 2.2 %convolution_convert_fusion.1 = bf16[256,256]{0,1:T(8,128)(2,1)S(1)} fusion(bf16[2048,256]{1,0:T(8,128)(2,1)} %param.16, bf16[256,2048]{1,0:T(8,128)(2,1)} %param.10, f32[2048]{0:T(1024)S(1)} %convert_element_type.73, f32[256]{0:T(256)S(1)} %add_rsqrt_fusion.2), kind=kOutput, calls=%fused_computation.30 | convolution fusion | flops 270598144 | bytes 2237440 | tf_op jit(solution)/shard_map/dot_general | solution.py:50
  10.0 0.7 copy.137
  10.8 0.6 convert_element_type.79
  11.3 2.6 %multiply_reduce_fusion.1 = (f32[256,2]{0,1:T(2,128)S(1)}, f32[256,256]{0,1:T(8,128)}) fusion(bf16[2048,256]{1,0:T(8,128)(2,1)} %param.15, bf16[256,2048]{1,0:T(8,128)(2,1)S(1)} %copy-done.3, f32[2048]{0:T(1024)S(1)} %convert_element_type.73, f32[256]{0:T(256)S(1)} %add_rsqrt_fusion.2), kind=kOutput, calls=%fused_computation.42 | convolution fusion | flops 270663168 | bytes 2370560 | tf_op jit(solution)/shard_map/dot_general | solution.py:47
  13.9 0.6 add_rsqrt_fusion.1
  14.5 0.1 convert_reduce_fusion
  14.6 0.8 scatter_custom_fusion
  15.4 0.6 select_reduce_fusion
  16.0 0.6 copy-done.7
  16.6 0.3 multiply_cosine_fusion
  17.0 0.1 copy.134
  17.1 1.1 multiply_multiply_fusion.1
  18.3 0.8 copy.156
  19.0 2.3 %fusion.29 = f32[256,512]{1,0:T(8,128)} fusion(bf16[2048,512]{1,0:T(8,128)(2,1)S(1)} %copy-done, bf16[256,2048]{1,0:T(8,128)(2,1)S(1)} %copy-done.3, f32[2048]{0:T(1024)} %copy-done.11, f32[256]{0:T(256)} %copy-done.16), kind=kOutput, calls=%fused_computation.107 | convolution fusion | flops 538968064 | bytes 3679232 | tf_op jit(solution)/shard_map/dot_general | solution.py:44
  21.3 1.2 reshape.469
  22.5 0.3 multiply_reduce_fusion
  22.9 0.3 multiply_multiply_fusion
  23.3 0.5 subtract_convert_fusion
  23.8 0.4 pad_maximum_fusion.1
  24.4 0.1 copy.131
  24.5 5.4 %gather_fusion = bf16[1024,1024]{1,0:T(8,128)(2,1)} fusion(bf16[256,1024]{1,0:T(8,128)(2,1)S(1)} %pad_maximum_fusion, s32[1024]{0:T(1024)S(1)} %broadcast_clamp_fusion), kind=kCustom, calls=%fused_computation | custom fusion | bytes 4198400 | tf_op jit(solution)/shard_map/jit(_take)/gather | solution.py:125
  29.9 4.0 %fusion.11 = bf16[16,64,1024]{2,0,1:T(8,128)(2,1)} fusion(bf16[16,64,1024]{2,1,0:T(8,128)(2,1)} %bitcast.64, pred[16,64]{0,1:T(8,128)(4,1)S(1)} %copy.131, pred[16,64]{0,1:T(8,128)(4,1)S(1)} %copy.130), kind=kLoop, calls=%fused_computation.25 | loop fusion | flops 2097152 | bytes 4196352 | tf_op jit(solution)/shard_map/jit(_where)/select_n | solution.py:127
  34.0 12.4 %all-to-all-start = ((bf16[16,64,1024]{2,0,1:T(8,128)(2,1)}), bf16[16,64,1024]{2,0,1:T(8,128)(2,1)}, u32[]{:S(2)}, u32[]{:S(2)}) async-start(bf16[16,64,1024]{2,0,1:T(8,128)(2,1)} %fusion.11), calls=%async_computation | async-start | bytes 4194304 | tf_op jit(solution)/shard_map/all_to_all | solution.py:126
  46.4 0.6 dynamic_slice.19
  48.9 0.6 dynamic_slice.21
  49.5 0.6 iota_compare_fusion.3
  50.2 1.3 fusion.6
  51.5 46.0 %all-to-all-done = bf16[16,64,1024]{2,0,1:T(8,128)(2,1)} async-done(((bf16[16,64,1024]{2,0,1:T(8,128)(2,1)}), bf16[16,64,1024]{2,0,1:T(8,128)(2,1)}, u32[]{:S(2)}, u32[]{:S(2)}) %all-to-all-start) | async-done | bytes 2097184 | tf_op jit(solution)/shard_map/all_to_all | solution.py:126
  97.5 2.7 %copy.139 = bf16[16,64,1024]{2,1,0:T(8,128)(2,1)S(1)} copy(bf16[16,64,1024]{2,0,1:T(8,128)(2,1)} %all-to-all-done) | data formatting | bytes 4194304 | tf_op jit(solution)/shard_map/all_to_all | solution.py:126
  100.2 1.6 fusion.10
  101.8 1.4 slice_bitcast_fusion
  103.3 0.1 slice.38
  103.4 2.0 %copy.141 = bf16[1024,256]{0,1:T(8,128)(2,1)} copy(bf16[1024,256]{1,0:T(8,128)(2,1)} %get-tuple-element.23) | data formatting | bytes 1048576 | tf_op jit(solution)/shard_map/slice | solution.py:136
  105.4 2.1 %copy.142 = bf16[1024,256]{0,1:T(8,128)(2,1)} copy(bf16[1024,256]{1,0:T(8,128)(2,1)} %get-tuple-element.22) | data formatting | bytes 1048576 | tf_op jit(solution)/shard_map/slice | solution.py:135
  107.5 1.3 copy.143
  108.8 11.2 %fusion.31 = (f32[2,2,1024]{2,1,0:T(2,128)S(1)}, f32[2,2,1024,1024]{2,3,1,0:T(8,128)}) fusion(pred[1024,1024]{0,1:T(8,128)(4,1)} %fusion.6, bf16[1024,2,128,1]{0,2,3,1:T(8,128)(2,1)} %bitcast.71, bf16[1024,2,2,128]{0,3,2,1:T(8,128)(2,1)} %bitcast.68), kind=kOutput, calls=%fused_computation.108 | convolution fusion | flops 1090520064 | bytes 19415040 | tf_op jit(solution)/shard_map/sub | solution.py:74
  120.0 7.2 %fusion.15 = bf16[1024,2,2,128]{0,3,2,1:T(8,128)(2,1)S(1)} fusion(bf16[1024,2,128,1]{0,2,3,1:T(8,128)(2,1)} %bitcast.70, f32[2,2,1024,1024]{2,3,1,0:T(8,128)} %get-tuple-element.35, f32[2,2,1024]{2,1,0:T(2,128)S(1)} %get-tuple-element.34), kind=kOutput, calls=%fused_computation.28 | convolution fusion | flops 1082654720 | bytes 18366464 | tf_op jit(solution)/shard_map/kgqs,skd->qkgd/dot_general | solution.py:76
  127.3 2.0 %copy.147 = bf16[1024,2,2,128]{3,2,1,0:T(2,128)(2,1)} copy(bf16[1024,2,2,128]{0,3,2,1:T(8,128)(2,1)S(1)} %fusion.15) | data formatting | bytes 2097152 | tf_op jit(solution)/shard_map/convert_element_type | solution.py:79
  129.3 1.5 reshape_reshape.3
  130.8 0.8 fusion.16
  131.6 1.5 copy.148
  133.1 5.6 %all-to-all-start.1 = ((bf16[16,64,512]{2,0,1:T(8,128)(2,1)}), bf16[16,64,512]{2,0,1:T(8,128)(2,1)}, u32[]{:S(2)}, u32[]{:S(2)}) async-start(bf16[16,64,512]{2,0,1:T(8,128)(2,1)} %copy.148), calls=%async_computation.1 | async-start | bytes 2097152 | tf_op jit(solution)/shard_map/all_to_all | solution.py:139
  138.9 28.6 %all-to-all-done.1 = bf16[16,64,512]{2,0,1:T(8,128)(2,1)} async-done(((bf16[16,64,512]{2,0,1:T(8,128)(2,1)}), bf16[16,64,512]{2,0,1:T(8,128)(2,1)}, u32[]{:S(2)}, u32[]{:S(2)}) %all-to-all-start.1) | async-done | bytes 1048608 | tf_op jit(solution)/shard_map/all_to_all | solution.py:139
  167.5 1.8 copy.149
  169.3 1.2 gather_fusion.1
  170.4 0.8 broadcast_select_fusion
  171.2 1.2 copy.150
  172.4 1.1 stack.16
  173.5 4.5 %all-to-all-start.2 = ((bf16[4,256,512]{1,2,0:T(8,128)(2,1)}), bf16[4,256,512]{1,2,0:T(8,128)(2,1)}, u32[]{:S(2)}, u32[]{:S(2)}) async-start(bf16[4,256,512]{1,2,0:T(8,128)(2,1)} %stack.16), calls=%async_computation.2 | async-start | bytes 2097152 | tf_op jit(solution)/shard_map/all_to_all | solution.py:13
  178.0 1.1 maximum_bitcast_fusion
  179.0 13.2 %all-to-all-done.2 = bf16[4,256,512]{1,2,0:T(8,128)(2,1)} async-done(((bf16[4,256,512]{1,2,0:T(8,128)(2,1)}), bf16[4,256,512]{1,2,0:T(8,128)(2,1)}, u32[]{:S(2)}, u32[]{:S(2)}) %all-to-all-start.2) | async-done | bytes 1048608 | tf_op jit(solution)/shard_map/all_to_all | solution.py:13
  192.2 2.6 %convolution_convert_fusion = bf16[256,512]{1,0:T(8,128)(2,1)S(1)} fusion(bf16[256,2048]{0,1:T(8,128)(2,1)} %bitcast.21, bf16[2048,512]{1,0:T(8,128)(2,1)} %param.19), kind=kOutput, calls=%fused_computation.29 | convolution fusion | flops 537001984 | bytes 3407872 | tf_op jit(solution)/shard_map/dot_general | solution.py:142
  194.9 1.7 add_convert_fusion
  (57 shorter events, 0.6 us)
Async XLA Ops:
  0.6 18.4 %copy-start = (bf16[2048,512]{1,0:T(8,128)(2,1)S(1)}, bf16[2048,512]{1,0:T(8,128)(2,1)}, u32[]{:S(2)}) copy-start(bf16[2048,512]{1,0:T(8,128)(2,1)} %param.14) | copy-start | bytes 6291460
  3.3 2.2 %copy-start.12 = (s32[64]{0:T(128)}, s32[64]{0:T(128)S(1)}, u32[]{:S(2)}) copy-start(s32[64]{0:T(128)S(1)} %get-tuple-element.19) | copy-start | bytes 772
  3.3 7.5 %copy-start.14 = (s32[64]{0:T(128)}, s32[64]{0:T(128)S(1)}, u32[]{:S(2)}) copy-start(s32[64]{0:T(128)S(1)} %get-tuple-element.18) | copy-start | bytes 772
  6.2 5.2 %copy-start.11 = (f32[2048]{0:T(1024)}, f32[2048]{0:T(1024)S(1)}, u32[]{:S(2)}) copy-start(f32[2048]{0:T(1024)S(1)} %convert_element_type.73) | copy-start | bytes 24580
  6.2 4.6 %copy-start.17 = (bf16[128]{0:T(256)(128)(2,1)S(1)}, bf16[128]{0:T(256)(128)(2,1)}, u32[]{:S(2)}) copy-start(bf16[128]{0:T(256)(128)(2,1)} %param.18) | copy-start | bytes 772
  6.2 5.2 %copy-start.3 = (bf16[256,2048]{1,0:T(8,128)(2,1)S(1)}, bf16[256,2048]{1,0:T(8,128)(2,1)}, u32[]{:S(2)}) copy-start(bf16[256,2048]{1,0:T(8,128)(2,1)} %param.10) | copy-start | bytes 3145732
  7.8 6.1 %copy-start.16 = (f32[256]{0:T(256)}, f32[256]{0:T(256)S(1)}, u32[]{:S(2)}) copy-start(f32[256]{0:T(256)S(1)} %add_rsqrt_fusion.2) | copy-start | bytes 3076
  16.0 0.6 copy-start.7
  19.0 3.5 %copy-start.18 = (bf16[128]{0:T(256)(128)(2,1)S(1)}, bf16[128]{0:T(256)(128)(2,1)}, u32[]{:S(2)}) copy-start(bf16[128]{0:T(256)(128)(2,1)} %param.17) | copy-start | bytes 772
  22.9 1.4 copy-start.6
  22.9 1.4 copy-start.10
  22.9 1.5 copy-start.4
  22.9 1.5 copy-start.5
  34.0 12.4 %copy-start.13 = (s32[64]{0:T(128)S(1)}, s32[64]{0:T(128)}, u32[]{:S(2)}) copy-start(s32[64]{0:T(128)} %copy-done.12) | copy-start | bytes 772
  34.0 15.0 %copy-start.15 = (s32[64]{0:T(128)S(1)}, s32[64]{0:T(128)}, u32[]{:S(2)}) copy-start(s32[64]{0:T(128)} %copy-done.14) | copy-start | bytes 772
  34.0 63.5 %all-to-all-start = ((bf16[16,64,1024]{2,0,1:T(8,128)(2,1)}), bf16[16,64,1024]{2,0,1:T(8,128)(2,1)}, u32[]{:S(2)}, u32[]{:S(2)}) async-start(bf16[16,64,1024]{2,0,1:T(8,128)(2,1)} %fusion.11), calls=%async_computation | async-start | bytes 4194304 | tf_op jit(solution)/shard_map/all_to_all | solution.py:126
  131.6 7.2 %copy-start.8 = (s32[256]{0:T(256)S(1)}, s32[256]{0:T(256)}, u32[]{:S(2)}) copy-start(s32[256]{0:T(256)} %copy-done.7) | copy-start | bytes 3076
  131.6 7.2 %copy-start.9 = (s32[256]{0:T(256)S(1)}, s32[256]{0:T(256)}, u32[]{:S(2)}) copy-start(s32[256]{0:T(256)} %get-tuple-element.16) | copy-start | bytes 3076
  133.1 34.3 %all-to-all-start.1 = ((bf16[16,64,512]{2,0,1:T(8,128)(2,1)}), bf16[16,64,512]{2,0,1:T(8,128)(2,1)}, u32[]{:S(2)}, u32[]{:S(2)}) async-start(bf16[16,64,512]{2,0,1:T(8,128)(2,1)} %copy.148), calls=%async_computation.1 | async-start | bytes 2097152 | tf_op jit(solution)/shard_map/all_to_all | solution.py:139
  171.2 6.7 %copy-start.1 = (bf16[1,1024,256]{2,1,0:T(8,128)(2,1)S(1)}, bf16[1,1024,256]{2,1,0:T(8,128)(2,1)}, u32[]{:S(2)}) copy-start(bf16[1,1024,256]{2,1,0:T(8,128)(2,1)} %get-tuple-element.20) | copy-start | bytes 1572868
  171.2 6.7 %copy-start.2 = (bf16[1,1024,256]{2,1,0:T(8,128)(2,1)S(1)}, bf16[1,1024,256]{2,1,0:T(8,128)(2,1)}, u32[]{:S(2)}) copy-start(bf16[1,1024,256]{2,1,0:T(8,128)(2,1)} %get-tuple-element.21) | copy-start | bytes 1572868
  173.5 18.7 %all-to-all-start.2 = ((bf16[4,256,512]{1,2,0:T(8,128)(2,1)}), bf16[4,256,512]{1,2,0:T(8,128)(2,1)}, u32[]{:S(2)}, u32[]{:S(2)}) async-start(bf16[4,256,512]{1,2,0:T(8,128)(2,1)} %stack.16), calls=%async_computation.2 | async-start | bytes 2097152 | tf_op jit(solution)/shard_map/all_to_all | solution.py:13
